TPU v7x, 32 devices: a whole 2x2x4 slice. The times are simulated.
32 devices in a mesh: dp: 4 (over y, x), expert: 8 (over z, core).
Axes of the slice: x: 2, y: 2, z: 4, core: 2. Of those that a mesh axis runs over, the one named last changes fastest.
Arguments:
- tokens: bfloat16 [4096, 2048], P(('dp', 'expert')), may hold values from -6 to 6
- cotangent: bfloat16 [4096, 2048], P(('dp', 'expert')), may hold values from -6 to 6
- expert_ids: int32 [4096, 4], P(('dp', 'expert')), may hold values from 0 to 7, all different within a row; in each aligned block of 128 rows (0 to 127, 128 to 255, ...) at most 96 rows name the same one
- gate_probs: float32 [4096, 4], P(('dp', 'expert')), may hold values from 0.05 to 1
- up_weight: bfloat16 [8, 2048, 768], P('expert', None, 'dp'), may hold values from -0.125 to 0.125
- down_weight: float32 [8, 768, 2048], P('expert', 'dp'), may hold values from -28 to 28
- moment1: float32 [8, 768, 2048], P('expert', 'dp'), may hold values from -60 to 60
- moment2: float32 [8, 768, 2048], P('expert', 'dp'), may hold values from 0.05 to 5
- pair_match: int32 [8], replicated, may hold values from 0 to 7, as said below
Outputs:
- down_out: float32 [8, 768, 2048], P('expert', 'dp')
- moment1_out: float32 [8, 768, 2048], P('expert', 'dp')
- moment2_out: float32 [8, 768, 2048], P('expert', 'dp')
Inputs may be any that keep to these rules, and one draw needn't show every extreme that they name: `expert_ids`: each row names 4 different experts. Within the rows of one device (aligned blocks of 128 rows) no expert is named by more than 96 rows, a bound that some block reaches. A perfect matching: pair_match[pair_match[i]] = i and pair_match[i] != i for every i.
All inputs are finite; a program needn't handle non-finite values.
Results may differ from a plain program's by a relative error of at most 0.00035.
Values may be sent and summed in bfloat16 or wider, within the bound.
No kernel may reach another device: no remote copies, remote signals or barrier semaphores. Data moves between devices by JAX's collectives and lax.ppermute only.
A program may use at most 128 MiB of HBM per device.

v0:
```python
import jax
import jax.numpy as jnp
from jax import lax
from jax.sharding import PartitionSpec as P

beta_one = 0.9
beta_two = 0.999
epsilon = 1e-06
learn_rate = 0.05


def relocate(states, pair_match):
    group_size = lax.axis_size("expert")
    count_states = len(states)
    stacked = jnp.stack(states).reshape(count_states, group_size, -1)
    chosen = jnp.take(
        lax.all_to_all(stacked, "expert", split_axis=1, concat_axis=1, tiled=True),
        pair_match,
        axis=1,
    )
    arrived = lax.all_to_all(chosen, "expert", split_axis=1, concat_axis=1, tiled=True)
    arrived = arrived.reshape((count_states,) + states[0].shape)
    return tuple((arrived[index] for index in range(count_states)))


def expert_gradient(tokens, cotangent, expert_ids, gate_probs, up_weight):
    group_size = lax.axis_size("expert")
    tok_rows, top_count = expert_ids.shape
    width = tokens.shape[1]
    capacity = 3 * tok_rows * top_count // (2 * group_size)
    total = tok_rows * top_count
    flat_ids = expert_ids.reshape(-1)
    picked = (flat_ids[:, None] == jnp.arange(group_size, dtype=jnp.int32)[None, :]).astype(
        jnp.int32
    )
    ranking = jnp.sum((jnp.cumsum(picked, axis=0) - 1) * picked, axis=1)
    slot_index = flat_ids * capacity + ranking
    source = (
        jnp.full((group_size * capacity,), total, jnp.int32)
        .at[slot_index]
        .set(jnp.arange(total, dtype=jnp.int32))
    )
    filled = source < total
    safe_source = jnp.minimum(source, total - 1)
    row_index = safe_source // top_count
    weights_row = jnp.where(filled, gate_probs.reshape(-1)[safe_source], jnp.float32(0.0))
    sent_tokens = jnp.where(filled[:, None], tokens[row_index], jnp.zeros((), jnp.bfloat16))
    sent_scaled = (weights_row[:, None] * cotangent[row_index].astype(jnp.float32)).astype(
        jnp.bfloat16
    )
    sent_tokens = sent_tokens.reshape(group_size, capacity, width)
    sent_scaled = sent_scaled.reshape(group_size, capacity, width)
    got_tokens, got_scaled = (
        lax.all_to_all(sent_tokens, "expert", split_axis=0, concat_axis=0, tiled=True),
        lax.all_to_all(sent_scaled, "expert", split_axis=0, concat_axis=0, tiled=True),
    )
    rows_tokens = got_tokens.reshape(-1, width)
    rows_scaled = got_scaled.reshape(-1, width)
    hidden = jax.nn.silu(
        jnp.dot(
            rows_tokens,
            lax.all_gather(up_weight[0], "dp", axis=1, tiled=True),
            preferred_element_type=jnp.float32,
        )
    ).astype(jnp.bfloat16)
    return lax.psum_scatter(
        lax.dot_general(
            hidden, rows_scaled, (((0,), (0,)), ((), ())), preferred_element_type=jnp.float32
        ),
        "dp",
        scatter_dimension=0,
        tiled=True,
    )


def lamb_step(weight, moment_one, moment_two, gradient):
    first = beta_one * moment_one + (1.0 - beta_one) * gradient
    second = beta_two * moment_two + (1.0 - beta_two) * gradient * gradient
    update = first / (jnp.sqrt(second) + epsilon)
    weight_sq, update_sq = lax.psum((jnp.sum(weight * weight), jnp.sum(update * update)), "dp")
    trust_ratio = jnp.sqrt(weight_sq) / (jnp.sqrt(update_sq) + epsilon)
    renewed = weight - learn_rate * trust_ratio * update
    return (renewed, first, second)


def local(
    tokens, cotangent, expert_ids, gate_probs, up_weight, down_weight, moment1, moment2, pair_match
):
    gradient = expert_gradient(tokens, cotangent, expert_ids, gate_probs, up_weight)
    renewed, first, second = lamb_step(down_weight[0], moment1[0], moment2[0], gradient)
    renewed, first, second = relocate((renewed, first, second), pair_match)
    return (renewed[None], first[None], second[None])


def solution(mesh):
    in_specs = (
        P(("dp", "expert"), None),
        P(("dp", "expert"), None),
        P(("dp", "expert"), None),
        P(("dp", "expert"), None),
        P("expert", None, "dp"),
        P("expert", "dp", None),
        P("expert", "dp", None),
        P("expert", "dp", None),
        P(),
    )
    out_specs = (P("expert", "dp", None), P("expert", "dp", None), P("expert", "dp", None))
    return jax.shard_map(local, mesh=mesh, in_specs=in_specs, out_specs=out_specs, check_vma=False)
```

profile of v0, /device:TPU:0, one launch (start us, length us, event | category | flops | bytes accessed | tf_op | source)
XLA Modules:
  0.0 632.6 jit_solution(5432400970827513326)
XLA Ops:
  7.2 0.8 copy.13
  8.0 0.1 eq.29
  8.1 0.1 eq.25
  8.2 0.7 broadcast_multiply_fusion
  8.9 1.1 reduce-window.6
  10.1 0.2 slice_reduce_fusion.3
  10.3 0.1 copy.12
  10.4 0.1 mul.85
  10.6 0.1 fusion.10
  10.7 2.4 scatter_custom_fusion
  13.1 0.8 copy.15
  13.9 0.1 reshape.103
  14.0 5.0 gather_fusion.1
  19.1 0.1 broadcast_in_dim.42
  19.2 4.3 gather_fusion
  23.5 3.8 broadcast_select_fusion
  27.3 6.5 %all-to-all-start = ((bf16[8,96,2048]{2,1,0:T(8,128)(2,1)}), bf16[8,96,2048]{2,1,0:T(8,128)(2,1)}, u32[]{:S(2)}, u32[]{:S(2)}) async-start(bf16[8,96,2048]{2,1,0:T(8,128)(2,1)} %broadcast_select_fusion), calls=%async_computation | async-start | bytes 6291456 | tf_op jit(solution)/shard_map/all_to_all | solution.py:54
  33.8 0.1 mul.88
  33.9 4.2 gather_fusion.2
  38.1 4.2 fusion
  42.3 63.1 %all-to-all-done = bf16[8,96,2048]{2,1,0:T(8,128)(2,1)} async-done(((bf16[8,96,2048]{2,1,0:T(8,128)(2,1)}), bf16[8,96,2048]{2,1,0:T(8,128)(2,1)}, u32[]{:S(2)}, u32[]{:S(2)}) %all-to-all-start) | async-done | bytes 3145760 | tf_op jit(solution)/shard_map/all_to_all | solution.py:54
  105.4 4.4 all-to-all-start.1
  109.8 0.0 all-gather.3.cloned.1.call-start
  109.9 0.7 all-gather.3.cloned.1.call-update
  110.6 0.2 reduce-scatter.2.cloned.1.call-start
  110.8 46.9 %all-gather.3.cloned.1.call-done = bf16[1,2048,768]{1,2,0:T(8,128)(2,1)} async-done(((bf16[1,2048,192]{1,2,0:T(8,128)(2,1)}), bf16[1,2048,768]{1,2,0:T(8,128)(2,1)}) %all-gather.3.cloned.1.call-update) | async-done | bytes 3145744 | tf_op jit(solution)/shard_map/all_gather | solution.py:62
  157.7 23.6 %all-to-all-done.1 = bf16[8,96,2048]{2,1,0:T(8,128)(2,1)} async-done(((bf16[8,96,2048]{2,1,0:T(8,128)(2,1)}), bf16[8,96,2048]{2,1,0:T(8,128)(2,1)}, u32[]{:S(2)}, u32[]{:S(2)}) %all-to-all-start.1) | async-done | bytes 3145760 | tf_op jit(solution)/shard_map/all_to_all | solution.py:55
  181.3 16.3 %fusion.8 = f32[768,2048]{1,0:T(8,128)} fusion(bf16[768,2048]{1,0:T(8,128)(2,1)} %bitcast.10, bf16[768,2048]{1,0:T(8,128)(2,1)} %bitcast.7, bf16[1,2048,768]{1,2,0:T(8,128)(2,1)} %all-gather.3.cloned.1.call-done), kind=kOutput, calls=%fused_computation.24 | convolution fusion | flops 4834787328 | bytes 15728640 | tf_op jit(solution)/shard_map/dot_general | solution.py:67
  197.6 0.0 reduce-scatter.2.cloned.1.call-update
  197.6 1.4 copy-done.3
  199.0 1.0 fusion.6
  200.0 66.7 %reduce-scatter.2.cloned.1.call-done = f32[192,2048]{1,0:T(8,128)} async-done(((f32[768,2048]{1,0:T(8,128)}), f32[192,2048]{1,0:T(8,128)}) %reduce-scatter.2.cloned.1.call-update) | async-done | bytes 1572880 | tf_op jit(solution)/shard_map/reduce_scatter | solution.py:66
  266.8 5.0 multiply_reduce_fusion
  271.8 9.8 %all-reduce = (f32[]{:T(128)}, f32[]{:T(128)}) all-reduce(f32[]{:T(128)} %fusion.6, f32[]{:T(128)} %get-tuple-element.8), channel_id=1, replica_groups=mesh['dp'=4,'expert'=8] {'dp'}, use_global_device_ids=true, to_apply=%region_1.2 | all-reduce | flops 2 | bytes 16 | tf_op jit(solution)/shard_map/psum | solution.py:80
  282.9 2.8 stack.17
  285.7 4.2 stack.18
  290.0 3.7 bitcast_subtract_fusion
  293.7 4.4 stack.16
  298.0 7.5 %pad_maximum_fusion = f32[3,8,49152]{2,0,1:T(4,128)} fusion(f32[1,8,49152]{2,0,1:T(1,128)} %stack.18, f32[1,8,49152]{2,0,1:T(1,128)S(1)} %copy-done.4, f32[1,8,49152]{2,0,1:T(1,128)} %stack.16), kind=kLoop, calls=%fused_computation.5 | loop fusion | flops 2359296 | bytes 9437184 | tf_op jit(solution)/shard_map/stack | solution.py:15
  305.5 4.9 all-to-all-start.2
  310.5 138.9 %all-to-all-done.2 = f32[3,8,49152]{2,0,1:T(4,128)} async-done(((f32[3,8,49152]{2,0,1:T(4,128)}), f32[3,8,49152]{2,0,1:T(4,128)}, u32[]{:S(2)}, u32[]{:S(2)}) %all-to-all-start.2) | async-done | bytes 4718624 | tf_op jit(solution)/shard_map/all_to_all | solution.py:17
  449.3 9.4 %gather_fusion.3 = f32[8,3,49152]{2,1,0:T(4,128)} fusion(f32[3,8,49152]{2,0,1:T(4,128)} %all-to-all-done.2, s32[1024]{0:T(1024)S(1)} %pad_clamp_fusion), kind=kCustom, calls=%fused_computation.3 | custom fusion | bytes 9437216 | tf_op jit(solution)/shard_map/jit(_take)/gather | solution.py:16
  458.7 4.4 select_bitcast_fusion
  463.1 141.4 %all_to_all.20 = f32[3,8,49152]{2,0,1:T(4,128)S(1)} all-to-all(f32[3,8,49152]{2,0,1:T(4,128)S(1)} %select_bitcast_fusion), channel_id=1, replica_groups=mesh['dp'=4,'expert'=8] {'expert'}, dimensions={1} | all-to-all | bytes 9437184 | tf_op jit(solution)/shard_map/all_to_all | solution.py:21
  604.5 14.1 %slice_reduce_fusion = (f32[8,49152]{1,0:T(8,128)S(1)}, f32[8,49152]{1,0:T(8,128)}, f32[8,49152]{1,0:T(8,128)}) fusion(f32[3,8,49152]{2,0,1:T(4,128)S(1)} %all_to_all.20), kind=kLoop, calls=%fused_computation.15 | loop fusion | bytes 9437184 | tf_op jit(solution)/shard_map/slice | solution.py:23
  618.6 2.8 slice.27
  621.5 2.8 slice.29
  624.3 1.4 slice.31
  (22 shorter events, 0.1 us)
Async XLA Ops:
  7.2 12.0 %copy-start = (bf16[128,2048]{1,0:T(8,128)(2,1)S(1)}, bf16[128,2048]{1,0:T(8,128)(2,1)}, u32[]{:S(2)}) copy-start(bf16[128,2048]{1,0:T(8,128)(2,1)} %param.9) | copy-start | bytes 1572868
  27.3 6.6 %copy-start.2 = (bf16[128,2048]{1,0:T(8,128)(2,1)S(1)}, bf16[128,2048]{1,0:T(8,128)(2,1)}, u32[]{:S(2)}) copy-start(bf16[128,2048]{1,0:T(8,128)(2,1)} %param.10) | copy-start | bytes 1572868
  27.3 78.1 %all-to-all-start = ((bf16[8,96,2048]{2,1,0:T(8,128)(2,1)}), bf16[8,96,2048]{2,1,0:T(8,128)(2,1)}, u32[]{:S(2)}, u32[]{:S(2)}) async-start(bf16[8,96,2048]{2,1,0:T(8,128)(2,1)} %broadcast_select_fusion), calls=%async_computation | async-start | bytes 6291456 | tf_op jit(solution)/shard_map/all_to_all | solution.py:54
  105.4 76.0 %all-to-all-start.1 = ((bf16[8,96,2048]{2,1,0:T(8,128)(2,1)}), bf16[8,96,2048]{2,1,0:T(8,128)(2,1)}, u32[]{:S(2)}, u32[]{:S(2)}) async-start(bf16[8,96,2048]{2,1,0:T(8,128)(2,1)} %fusion), calls=%async_computation.1 | async-start | bytes 6291456 | tf_op jit(solution)/shard_map/all_to_all | solution.py:55
  109.8 47.9 %all-gather.3.cloned.1.call-start = ((), (), s32[]{:S(2)}) async-start(), calls=%async_computation.6 | async-start | bytes 3932160 | tf_op jit(solution)/shard_map/all_gather | solution.py:62
  110.6 156.2 %reduce-scatter.2.cloned.1.call-start = ((), (), s32[]{:S(2)}) async-start(), calls=%async_computation.5 | async-start | bytes 7864320 | tf_op jit(solution)/shard_map/reduce_scatter | solution.py:66
  197.6 1.4 copy-start.3
  293.7 4.4 copy-start.4
  305.5 4.9 copy-start.5
  305.5 143.8 %all-to-all-start.2 = ((f32[3,8,49152]{2,0,1:T(4,128)}), f32[3,8,49152]{2,0,1:T(4,128)}, u32[]{:S(2)}, u32[]{:S(2)}) async-start(f32[3,8,49152]{2,0,1:T(4,128)} %pad_maximum_fusion), calls=%async_computation.3 | async-start | bytes 12582912 | tf_op jit(solution)/shard_map/all_to_all | solution.py:17
  624.3 1.4 copy-start.1
Sparse Core Ops, SparseCore 0:
  112.5 45.1 all-gather.2
  197.8 68.9 reduce-scatter.1
where the time goes:
time: 633 us
  waiting for transfers between devices  340 us (54%)
  blocking collectives  151 us (24%)
  local copies, waits for them, and re-layouts  61.9 us (10%)
  other arithmetic  31.6 us (5%)
  matrix products  16.3 us (3%)
  starting transfers between devices  16.1 us (3%)
  between operations  15.6 us (2%)
    all_to_all x1, blocking collectives, relocate(): lax.all_to_all(chosen, 'expert', split_axis=1, concat_axis=1, tiled=True)  141 us
    all_to_all x1, waiting for transfers between devices, relocate(): lax.all_to_all(stacked, 'expert', split_axis=1, concat_axis=1, tiled=True)  139 us
    reduce_scatter x1, waiting for transfers between devices, expert_gradient(): lax.psum_scatter(lax.dot_general(hidden, rows_scaled, (((0,), (0,)), ((),...  66.7 us
    all_to_all x1, waiting for transfers between devices, expert_gradient(): lax.all_to_all(sent_tokens, 'expert', split_axis=0, concat_axis=0, tiled=...  63.1 us
    all_gather x1, waiting for transfers between devices, expert_gradient(): lax.all_gather(up_weight[0], 'dp', axis=1, tiled=True)  46.9 us
    all_to_all x1, waiting for transfers between devices, expert_gradient(): lax.all_to_all(sent_scaled, 'expert', split_axis=0, concat_axis=0, tiled=...  23.6 us
    slice x4, local copies, waits for them, and re-layouts, relocate(): return tuple((arrived[index] for index in range(count_states)))  21.2 us
    dot_general x1, matrix products, expert_gradient(): lax.dot_general(hidden, rows_scaled, (((0,), (0,)), ((), ())), preferred_...  16.3 us
  transfers between devices with their start and end apart: 5, of which 5 were waited for; matrix products, arithmetic and copies ran while one was open for 1% of the time, Pallas kernels for 0%

commit v1 on v0

--- a/solution.py
+++ b/solution.py
@@ -7,6 +7,28 @@
 beta_two = 0.999
 epsilon = 1e-06
 learn_rate = 0.05
+
+
+def cut_along(value, dim, size):
+    before, after = (value.shape[:dim], value.shape[dim + 1 :])
+    return jnp.moveaxis(value.reshape(*before, size, -1, *after), dim, 0)
+
+
+def in_order(blocks, dim):
+    blocks = jnp.moveaxis(blocks, 0, dim)
+    lengths = blocks.shape
+    return blocks.reshape(*lengths[:dim], lengths[dim] * lengths[dim + 1], *lengths[dim + 2 :])
+
+
+def exchange_in_pairs(x, axis, split_dim, concat_dim):
+    count, index = (lax.axis_size(axis), lax.axis_index(axis))
+    pieces = cut_along(x, split_dim, count)
+    outs = [pieces[index]]
+    for step in range(1, count):
+        sent = pieces[index ^ step]
+        outs.append(lax.ppermute(sent, axis, [(i, i ^ step) for i in range(count)]))
+    pieces = jnp.stack(outs)[index ^ jnp.arange(count)]
+    return in_order(pieces, concat_dim)
 
 
 def relocate(states, pair_match):
@@ -51,7 +73,7 @@
     sent_tokens = sent_tokens.reshape(group_size, capacity, width)
     sent_scaled = sent_scaled.reshape(group_size, capacity, width)
     got_tokens, got_scaled = (
-        lax.all_to_all(sent_tokens, "expert", split_axis=0, concat_axis=0, tiled=True),
+        exchange_in_pairs(sent_tokens, "expert", 0, 0),
         lax.all_to_all(sent_scaled, "expert", split_axis=0, concat_axis=0, tiled=True),
     )
     rows_tokens = got_tokens.reshape(-1, width)

time: 633 us -> 629 us (level)
  waiting for transfers between devices: 340 us -> 320 us
  local copies, waits for them, and re-layouts: 61.9 us -> 72.7 us
    ppermute x0 -> x7, waiting for transfers between devices: none -> 99 us  [exchange_in_pairs(): outs.append(lax.ppermute(sent, axis, [(i, i ^ step) for i in range(count)]))]
    all_to_all x1 -> x0, waiting for transfers between devices: 63.1 us -> none  [expert_gradient(): lax.all_to_all(sent_tokens, 'expert', split_axis=0, concat_axis=0, tiled=...]
    all_gather x1, waiting for transfers between devices: 46.9 us -> 0.01 us  [expert_gradient(): lax.all_gather(up_weight[0], 'dp', axis=1, tiled=True)]
    all_to_all x1, waiting for transfers between devices: 23.6 us -> 0.01 us  [expert_gradient(): lax.all_to_all(sent_scaled, 'expert', split_axis=0, concat_axis=0, tiled=...]
    reduce_scatter x1, waiting for transfers between devices: 66.7 us -> 81.7 us  [expert_gradient(): lax.psum_scatter(lax.dot_general(hidden, rows_scaled, (((0,), (0,)), ((),...]
    ppermute x0 -> x7, starting transfers between devices: none -> 10.8 us  [exchange_in_pairs(): outs.append(lax.ppermute(sent, axis, [(i, i ^ step) for i in range(count)]))]
    all_to_all x1 -> x0, starting transfers between devices: 6.49 us -> none  [expert_gradient(): lax.all_to_all(sent_tokens, 'expert', split_axis=0, concat_axis=0, tiled=...]
  transfers between devices with their start and end apart: 5 -> 11, of which waited for: 5 -> 6; matrix products, arithmetic and copies ran while one was open for 1% -> 3% of each run, Pallas kernels for 0% -> 0%
where the time goes in v1:
time: 629 us; the launch traced here: 628 us
  waiting for transfers between devices  320 us (51%)
  blocking collectives  151 us (24%)
  local copies, waits for them, and re-layouts  72.7 us (12%)
  other arithmetic  29.9 us (5%)
  starting transfers between devices  22.4 us (4%)
  matrix products  16.3 us (3%)
  between operations  15.7 us (2%)
    all_to_all x1, blocking collectives, relocate(): lax.all_to_all(chosen, 'expert', split_axis=1, concat_axis=1, tiled=True)  141 us
    all_to_all x1, waiting for transfers between devices, relocate(): lax.all_to_all(stacked, 'expert', split_axis=1, concat_axis=1, tiled=True)  139 us
    ppermute x7, waiting for transfers between devices, exchange_in_pairs(): outs.append(lax.ppermute(sent, axis, [(i, i ^ step) for i in range(count)]))  99 us
    reduce_scatter x1, waiting for transfers between devices, expert_gradient(): lax.psum_scatter(lax.dot_general(hidden, rows_scaled, (((0,), (0,)), ((),...  81.7 us
    slice x4, local copies, waits for them, and re-layouts, relocate(): return tuple((arrived[index] for index in range(count_states)))  21.2 us
    dot_general x1, matrix products, expert_gradient(): lax.dot_general(hidden, rows_scaled, (((0,), (0,)), ((), ())), preferred_...  16.3 us
  transfers between devices with their start and end apart: 11, of which 6 were waited for; matrix products, arithmetic and copies ran while one was open for 3% of the time, Pallas kernels for 0%

profile of v1, /device:TPU:0, one launch (start us, length us, event | category | flops | bytes accessed | tf_op | source)
XLA Modules:
  0.0 628.5 jit_solution(11384201023638721064)
XLA Ops:
  7.2 0.8 copy.13
  8.2 0.7 broadcast_multiply_fusion
  8.9 1.1 reduce-window.6
  10.7 2.4 scatter_custom_fusion
  13.1 0.8 copy.15
  14.0 5.0 gather_fusion.2
  19.1 4.3 gather_fusion.3
  23.4 4.1 fusion
  27.6 6.5 %all-to-all-start = ((bf16[8,96,2048]{2,1,0:T(8,128)(2,1)}), bf16[8,96,2048]{2,1,0:T(8,128)(2,1)}, u32[]{:S(2)}, u32[]{:S(2)}) async-start(bf16[8,96,2048]{2,1,0:T(8,128)(2,1)} %fusion), calls=%async_computation | async-start | bytes 6291456 | tf_op jit(solution)/shard_map/all_to_all | solution.py:77
  35.1 4.3 gather_fusion
  39.4 2.2 broadcast_select_fusion
  41.6 1.0 dynamic-slice_bitcast_fusion
  43.1 1.6 collective-permute-start.1
  44.7 2.6 collective-permute-start.3
  47.5 3.5 collective-permute-start.5
  51.0 0.8 bitcast_dynamic-update-slice_fusion.6
  51.8 42.6 %collective-permute-done.1 = bf16[1,96,2048]{2,1,0:T(8,128)(2,1)S(1)} collective-permute-done((bf16[1,96,2048]{2,1,0:T(8,128)(2,1)S(1)}, bf16[1,96,2048]{2,1,0:T(8,128)(2,1)S(1)}, u32[]{:S(2)}, u32[]{:S(2)}) %collective-permute-start.1) | collective-permute-done | bytes 393248 | tf_op jit(solution)/shard_map/ppermute | solution.py:29
  94.4 2.4 collective-permute-start.6
  96.8 0.8 bitcast_dynamic-update-slice_fusion.5
  97.6 5.2 collective-permute-done.2
  102.8 0.8 bitcast_dynamic-update-slice_fusion.4
  103.6 44.7 %collective-permute-done.3 = bf16[1,96,2048]{2,1,0:T(8,128)(2,1)S(1)} collective-permute-done((bf16[1,96,2048]{2,1,0:T(8,128)(2,1)S(1)}, bf16[1,96,2048]{2,1,0:T(8,128)(2,1)S(1)}, u32[]{:S(2)}, u32[]{:S(2)}) %collective-permute-start.3) | collective-permute-done | bytes 393248 | tf_op jit(solution)/shard_map/ppermute | solution.py:29
  148.3 0.8 bitcast_dynamic-update-slice_fusion.3
  149.1 6.5 %collective-permute-done.4 = bf16[1,96,2048]{2,1,0:T(8,128)(2,1)S(1)} collective-permute-done((bf16[1,96,2048]{2,1,0:T(8,128)(2,1)S(1)}, bf16[1,96,2048]{2,1,0:T(8,128)(2,1)S(1)}, u32[]{:S(2)}, u32[]{:S(2)}) %collective-permute-start.4) | collective-permute-done | bytes 393248 | tf_op jit(solution)/shard_map/ppermute | solution.py:29
  155.5 0.8 bitcast_dynamic-update-slice_fusion.2
  156.3 0.8 bitcast_dynamic-update-slice_fusion.1
  157.1 0.8 bitcast_dynamic-update-slice_fusion
  157.9 4.3 gather_fusion.1
  162.2 16.3 %fusion.8 = f32[768,2048]{1,0:T(8,128)} fusion(bf16[768,2048]{1,0:T(8,128)(2,1)} %bitcast.26, bf16[768,2048]{1,0:T(8,128)(2,1)} %bitcast.68, bf16[1,2048,768]{1,2,0:T(8,128)(2,1)} %all-gather.3.cloned.1.call-done), kind=kOutput, calls=%fused_computation.25 | convolution fusion | flops 4834787328 | bytes 15728640 | tf_op jit(solution)/shard_map/dot_general | solution.py:89
  178.5 1.4 copy-done.3
  179.9 1.0 fusion.6
  180.9 81.7 %reduce-scatter.2.cloned.1.call-done = f32[192,2048]{1,0:T(8,128)} async-done(((f32[768,2048]{1,0:T(8,128)}), f32[192,2048]{1,0:T(8,128)}) %reduce-scatter.2.cloned.1.call-update) | async-done | bytes 1572880 | tf_op jit(solution)/shard_map/reduce_scatter | solution.py:88
  262.6 5.0 multiply_reduce_fusion
  267.6 9.8 %all-reduce = (f32[]{:T(128)}, f32[]{:T(128)}) all-reduce(f32[]{:T(128)} %fusion.6, f32[]{:T(128)} %get-tuple-element.8), channel_id=1, replica_groups=mesh['dp'=4,'expert'=8] {'dp'}, use_global_device_ids=true, to_apply=%region_1.2 | all-reduce | flops 2 | bytes 16 | tf_op jit(solution)/shard_map/psum | solution.py:102
  278.8 2.8 stack.49
  281.6 4.2 stack.50
  285.8 3.7 bitcast_subtract_fusion
  289.5 4.4 stack.48
  293.9 7.5 %pad_maximum_fusion = f32[3,8,49152]{2,0,1:T(4,128)} fusion(f32[1,8,49152]{2,0,1:T(1,128)} %stack.50, f32[1,8,49152]{2,0,1:T(1,128)S(1)} %copy-done.4, f32[1,8,49152]{2,0,1:T(1,128)} %stack.48), kind=kLoop, calls=%fused_computation.6 | loop fusion | flops 2359296 | bytes 9437184 | tf_op jit(solution)/shard_map/stack | solution.py:37
  301.4 4.9 all-to-all-start.1
  306.3 138.9 %all-to-all-done.1 = f32[3,8,49152]{2,0,1:T(4,128)} async-done(((f32[3,8,49152]{2,0,1:T(4,128)}), f32[3,8,49152]{2,0,1:T(4,128)}, u32[]{:S(2)}, u32[]{:S(2)}) %all-to-all-start.1) | async-done | bytes 4718624 | tf_op jit(solution)/shard_map/all_to_all | solution.py:39
  445.2 9.4 %gather_fusion.4 = f32[8,3,49152]{2,1,0:T(4,128)} fusion(f32[3,8,49152]{2,0,1:T(4,128)} %all-to-all-done.1, s32[1024]{0:T(1024)S(1)} %pad_clamp_fusion), kind=kCustom, calls=%fused_computation.4 | custom fusion | bytes 9437216 | tf_op jit(solution)/shard_map/jit(_take)/gather | solution.py:38
  454.5 4.4 select_bitcast_fusion
  458.9 141.4 %all_to_all.15 = f32[3,8,49152]{2,0,1:T(4,128)S(1)} all-to-all(f32[3,8,49152]{2,0,1:T(4,128)S(1)} %select_bitcast_fusion), channel_id=1, replica_groups=mesh['dp'=4,'expert'=8] {'expert'}, dimensions={1} | all-to-all | bytes 9437184 | tf_op jit(solution)/shard_map/all_to_all | solution.py:43
  600.4 14.1 %slice_reduce_fusion = (f32[8,49152]{1,0:T(8,128)S(1)}, f32[8,49152]{1,0:T(8,128)}, f32[8,49152]{1,0:T(8,128)}) fusion(f32[3,8,49152]{2,0,1:T(4,128)S(1)} %all_to_all.15), kind=kLoop, calls=%fused_computation.16 | loop fusion | bytes 9437184 | tf_op jit(solution)/shard_map/slice | solution.py:45
  614.5 2.8 slice.27
  617.3 2.9 slice.29
  620.2 1.4 slice.31
  (45 shorter events, 2.7 us)
Async XLA Ops:
  7.2 12.0 %copy-start = (bf16[128,2048]{1,0:T(8,128)(2,1)S(1)}, bf16[128,2048]{1,0:T(8,128)(2,1)}, u32[]{:S(2)}) copy-start(bf16[128,2048]{1,0:T(8,128)(2,1)} %param.10) | copy-start | bytes 1572868
  27.6 7.6 %copy-start.2 = (bf16[128,2048]{1,0:T(8,128)(2,1)S(1)}, bf16[128,2048]{1,0:T(8,128)(2,1)}, u32[]{:S(2)}) copy-start(bf16[128,2048]{1,0:T(8,128)(2,1)} %param.9) | copy-start | bytes 1572868
  27.6 134.7 %all-to-all-start = ((bf16[8,96,2048]{2,1,0:T(8,128)(2,1)}), bf16[8,96,2048]{2,1,0:T(8,128)(2,1)}, u32[]{:S(2)}, u32[]{:S(2)}) async-start(bf16[8,96,2048]{2,1,0:T(8,128)(2,1)} %fusion), calls=%async_computation | async-start | bytes 6291456 | tf_op jit(solution)/shard_map/all_to_all | solution.py:77
  34.1 128.2 %all-gather.3.cloned.1.call-start = ((), (), s32[]{:S(2)}) async-start(), calls=%async_computation.5 | async-start | bytes 3932160 | tf_op jit(solution)/shard_map/all_gather | solution.py:84
  34.8 227.8 %reduce-scatter.2.cloned.1.call-start = ((), (), s32[]{:S(2)}) async-start(), calls=%async_computation.4 | async-start | bytes 7864320 | tf_op jit(solution)/shard_map/reduce_scatter | solution.py:88
  42.6 4.9 collective-permute-start
  43.1 51.3 %collective-permute-start.1 = (bf16[1,96,2048]{2,1,0:T(8,128)(2,1)S(1)}, bf16[1,96,2048]{2,1,0:T(8,128)(2,1)S(1)}, u32[]{:S(2)}, u32[]{:S(2)}) collective-permute-start(bf16[1,96,2048]{2,1,0:T(8,128)(2,1)S(1)} %get-tuple-element.18), channel_id=1, source_target_pairs={{0,2},{1,3},{2,0},{3,1},{4,6},{5,7},{6,4},{7,5},{8,10},{9,11},{10,... | collective-permute-start | bytes 1179656 | tf_op jit(solution)/shard_map/ppermute | solution.py:29
  44.7 58.1 %collective-permute-start.2 = (bf16[1,96,2048]{2,1,0:T(8,128)(2,1)S(1)}, bf16[1,96,2048]{2,1,0:T(8,128)(2,1)S(1)}, u32[]{:S(2)}, u32[]{:S(2)}) collective-permute-start(bf16[1,96,2048]{2,1,0:T(8,128)(2,1)S(1)} %get-tuple-element.17), channel_id=1, source_target_pairs={{0,3},{1,2},{2,1},{3,0},{4,7},{5,6},{6,5},{7,4},{8,11},{9,10},{10,... | collective-permute-start | bytes 1179656 | tf_op jit(solution)/shard_map/ppermute | solution.py:29
  44.7 103.5 %collective-permute-start.3 = (bf16[1,96,2048]{2,1,0:T(8,128)(2,1)S(1)}, bf16[1,96,2048]{2,1,0:T(8,128)(2,1)S(1)}, u32[]{:S(2)}, u32[]{:S(2)}) collective-permute-start(bf16[1,96,2048]{2,1,0:T(8,128)(2,1)S(1)} %get-tuple-element.16), channel_id=1, source_target_pairs={{0,4},{1,5},{2,6},{3,7},{4,0},{5,1},{6,2},{7,3},{8,12},{9,13},{10,... | collective-permute-start | bytes 1179656 | tf_op jit(solution)/shard_map/ppermute | solution.py:29
  47.4 108.2 %collective-permute-start.4 = (bf16[1,96,2048]{2,1,0:T(8,128)(2,1)S(1)}, bf16[1,96,2048]{2,1,0:T(8,128)(2,1)S(1)}, u32[]{:S(2)}, u32[]{:S(2)}) collective-permute-start(bf16[1,96,2048]{2,1,0:T(8,128)(2,1)S(1)} %get-tuple-element.15), channel_id=1, source_target_pairs={{0,5},{1,4},{2,7},{3,6},{4,1},{5,0},{6,3},{7,2},{8,13},{9,12},{10,... | collective-permute-start | bytes 1179656 | tf_op jit(solution)/shard_map/ppermute | solution.py:29
  47.5 108.8 %collective-permute-start.5 = (bf16[1,96,2048]{2,1,0:T(8,128)(2,1)S(1)}, bf16[1,96,2048]{2,1,0:T(8,128)(2,1)S(1)}, u32[]{:S(2)}, u32[]{:S(2)}) collective-permute-start(bf16[1,96,2048]{2,1,0:T(8,128)(2,1)S(1)} %get-tuple-element.14), channel_id=1, source_target_pairs={{0,6},{1,7},{2,4},{3,5},{4,2},{5,3},{6,0},{7,1},{8,14},{9,15},{10,... | collective-permute-start | bytes 1179656 | tf_op jit(solution)/shard_map/ppermute | solution.py:29
  94.4 62.8 %collective-permute-start.6 = (bf16[1,96,2048]{2,1,0:T(8,128)(2,1)S(1)}, bf16[1,96,2048]{2,1,0:T(8,128)(2,1)S(1)}, u32[]{:S(2)}, u32[]{:S(2)}) collective-permute-start(bf16[1,96,2048]{2,1,0:T(8,128)(2,1)S(1)} %get-tuple-element.13), channel_id=1, source_target_pairs={{0,7},{1,6},{2,5},{3,4},{4,3},{5,2},{6,1},{7,0},{8,15},{9,14},{10,... | collective-permute-start | bytes 1179656 | tf_op jit(solution)/shard_map/ppermute | solution.py:29
  178.5 1.4 copy-start.3
  289.5 4.4 copy-start.4
  301.4 4.9 copy-start.5
  301.4 143.8 %all-to-all-start.1 = ((f32[3,8,49152]{2,0,1:T(4,128)}), f32[3,8,49152]{2,0,1:T(4,128)}, u32[]{:S(2)}, u32[]{:S(2)}) async-start(f32[3,8,49152]{2,0,1:T(4,128)} %pad_maximum_fusion), calls=%async_computation.2 | async-start | bytes 12582912 | tf_op jit(solution)/shard_map/all_to_all | solution.py:39
  617.3 4.3 copy-start.1
Sparse Core Ops, SparseCore 0:
  36.7 45.2 all-gather.2
  178.7 83.8 reduce-scatter.1
